TPU v7x, 256 devices: a whole 4x4x8 slice. The times are simulated.
256 devices in a mesh: feat: 64 (over x, z, core), rep: 4 (over y).
Axes of the slice: x: 4, y: 4, z: 8, core: 2. Of those that a mesh axis runs over, the one named last changes fastest.
Arguments:
- features: bfloat16 [4, 128, 32768], P('rep', 'feat'), may hold values from -6 to 6
- neighbors_one: int32 [4, 15, 16384], P('rep'), may hold values from 0 to 32767, as said below
- weight_one: bfloat16 [2, 128, 256], P(None, 'feat'), may hold values from -0.375 to 0.375
- weight_two: bfloat16 [2, 256, 256], replicated, may hold values from -0.25 to 0.25
- send_rows: int32 [4, 64, 64, 32], P('rep', 'feat'), may hold values from 0 to 255
- halo_count: int32 [4, 64, 64], P('rep', 'feat'), may hold values from 1 to 32, as said below
- neighbors_two: int32 [4, 10, 16384], P('rep', None, 'feat'), may hold values from 0 to 2303, as said below
- cotangent: bfloat16 [4, 16384, 256], P('rep', 'feat'), may hold values from -6 to 6
Outputs:
- hidden_two: bfloat16 [4, 16384, 256], P('rep', 'feat')
- grad_one: float32 [2, 128, 256], P(None, 'feat')
- grad_two: float32 [2, 256, 256], replicated
Inputs may be any that keep to these rules, and one draw needn't show every extreme that they name: neighbors_one[r, k, v] lies in the block of sources from 2 * 512 * (v // 512) to 2 * 512 * (v // 512) + 2 * 512 - 1. halo_count[r, p, q] is how many halo slots shard p fills for shard q; in every replica one shard q receives exactly 32 from every shard, every other count is at most 24. send_rows[r, p, q, j] is a local row of shard p; entries with j >= halo_count[r, p, q] are ignored. `neighbors_two`: an entry below 256 is a local row; an entry 256 + p * 32 + j is a halo slot with j < halo_count[r, p, q] for the seed's shard q; every such live slot is named at least once on its shard.
All inputs are finite; a program needn't handle non-finite values.
Results may differ from a plain program's by a relative error of at most 0.0051.
Values may be sent and summed in bfloat16 or wider, within the bound.
No kernel may reach another device: no remote copies, remote signals or barrier semaphores. Data moves between devices by JAX's collectives and lax.ppermute only.
A program may use at most 64 MiB of HBM per device.

v0:
```python
import math
import jax
import jax.numpy as jnp
from jax import lax
from jax.sharding import PartitionSpec as P

BLOCK_NODES = 512


def activate(pre):
    return jnp.where(pre > 0.0, pre, jnp.expm1(jnp.minimum(pre, 0.0)))


def elu_slope(pre):
    return jnp.where(pre > 0.0, jnp.ones_like(pre), jnp.exp(jnp.minimum(pre, 0.0)))


def to_nodes(stacked):
    return lax.all_to_all(stacked, "feat", split_axis=2, concat_axis=1, tiled=True)


def block_aggregate(table_x, index_one):
    columns = table_x.shape[0]
    fanout_one = index_one.shape[0]
    layer_rows = index_one.shape[1]
    block_rows = BLOCK_NODES
    span_width = 2 * block_rows
    blocks_total = layer_rows // block_rows
    group_size = math.gcd(blocks_total, 4)
    turn_count = blocks_total // group_size
    table_parts = jnp.transpose(
        table_x.reshape(columns, turn_count, group_size, span_width), (1, 0, 2, 3)
    )
    block_base = (jnp.arange(blocks_total, dtype=jnp.int32) * span_width).reshape(
        turn_count, group_size
    )
    relative = (
        index_one.reshape(fanout_one, turn_count, group_size, block_rows)
        - block_base[None, :, :, None]
    )
    relative = jnp.transpose(relative, (1, 0, 2, 3))

    def one_turn(pair):
        table_part, relative_part = pair
        positions = lax.broadcasted_iota(jnp.int32, (group_size, block_rows, span_width), 2)
        tallies = jnp.zeros((group_size, block_rows, span_width), jnp.bfloat16)
        for sample in range(fanout_one):
            tallies = tallies + (relative_part[sample][:, :, None] == positions).astype(
                jnp.bfloat16
            )
        summed = jnp.einsum("cgs,gvs->cgv", table_part, tallies, preferred_element_type=jnp.float32)
        return (summed / fanout_one).astype(jnp.bfloat16)

    gathered = lax.map(one_turn, (table_parts, relative))
    return jnp.transpose(gathered, (1, 0, 2, 3)).reshape(columns, layer_rows)


def on_device(
    features, neighbors_one, weight_one, weight_two, send_rows, halo_count, neighbors_two, cotangent
):
    feat_devs = lax.axis_size("feat")
    rep_devs = lax.axis_size("rep")
    table_x = features[0]
    index_one = neighbors_one[0]
    layer_rows = index_one.shape[1]
    node_count = layer_rows // feat_devs
    hidden_width = weight_one.shape[2]
    aggregate_one = block_aggregate(table_x, index_one)
    stacked = jnp.stack([table_x[:, :layer_rows], aggregate_one])
    node_feats = None
    node_feats = to_nodes(stacked)
    full_weight = lax.all_gather(weight_one, "feat", axis=1, tiled=True)
    pre_one = jnp.einsum("sfr,sfh->rh", node_feats, full_weight, preferred_element_type=jnp.float32)
    hidden_one = activate(pre_one).astype(jnp.bfloat16)
    send_slots = send_rows[0, 0]
    counts = halo_count[0, 0]
    capacity = send_slots.shape[1]
    live_slots = lax.broadcasted_iota(jnp.int32, send_slots.shape, 1) < counts[:, None]
    outgoing = jnp.where(
        live_slots[:, :, None], hidden_one[send_slots], jnp.zeros((), jnp.bfloat16)
    )
    incoming = lax.all_to_all(outgoing, "feat", split_axis=0, concat_axis=0, tiled=True)
    table_two = jnp.concatenate(
        [hidden_one, incoming.reshape(feat_devs * capacity, hidden_width)], axis=0
    )
    index_two = neighbors_two[0]
    fanout_two = index_two.shape[0]
    seed_rows = index_two.shape[1]
    summed_two = jnp.zeros((seed_rows, hidden_width), jnp.float32)
    for sample in range(fanout_two):
        summed_two = summed_two + table_two[index_two[sample]].astype(jnp.float32)
    aggregate_two = (summed_two / fanout_two).astype(jnp.bfloat16)
    pre_two = jnp.dot(hidden_one, weight_two[0], preferred_element_type=jnp.float32) + jnp.dot(
        aggregate_two, weight_two[1], preferred_element_type=jnp.float32
    )
    hidden_two = activate(pre_two).astype(jnp.bfloat16)
    grad_scale = 1.0 / math.sqrt(rep_devs * feat_devs * seed_rows)
    slope_two = (cotangent[0].astype(jnp.float32) * elu_slope(pre_two) * grad_scale).astype(
        jnp.bfloat16
    )
    local_two = jnp.stack(
        [
            jnp.einsum("rh,rk->hk", hidden_one, slope_two, preferred_element_type=jnp.float32),
            jnp.einsum("rh,rk->hk", aggregate_two, slope_two, preferred_element_type=jnp.float32),
        ]
    )
    grad_two = lax.psum(local_two, ("feat", "rep"))
    back_self = jnp.einsum(
        "rk,hk->rh", slope_two, weight_two[0], preferred_element_type=jnp.float32
    )
    back_agg = (
        jnp.einsum("rk,hk->rh", slope_two, weight_two[1], preferred_element_type=jnp.float32)
        / fanout_two
    )
    grad_table = jnp.zeros((table_two.shape[0], hidden_width), jnp.float32)
    for sample in range(fanout_two):
        grad_table = grad_table.at[index_two[sample]].add(back_agg)
    grad_table = grad_table.at[:seed_rows].add(back_self)
    returned = lax.all_to_all(
        grad_table[node_count:].reshape(feat_devs, capacity, hidden_width).astype(jnp.bfloat16),
        "feat",
        split_axis=0,
        concat_axis=0,
        tiled=True,
    ).astype(jnp.float32)
    returned = jnp.where(live_slots[:, :, None], returned, 0.0)
    back_one = grad_table[:node_count].at[send_slots].add(returned)
    slope_one = (back_one * elu_slope(pre_one)).astype(jnp.bfloat16)
    first_local = jnp.einsum(
        "scr,rh->sch",
        stacked,
        lax.all_gather(slope_one, "feat", axis=0, tiled=True),
        preferred_element_type=jnp.float32,
    )
    grad_one = lax.psum(first_local, "rep")
    return (hidden_two[None], grad_one, grad_two)


def solution(mesh):
    return jax.shard_map(
        on_device,
        mesh=mesh,
        in_specs=(
            P("rep", "feat", None),
            P("rep", None, None),
            P(None, "feat", None),
            P(),
            P("rep", "feat", None, None),
            P("rep", "feat", None),
            P("rep", None, "feat"),
            P("rep", "feat", None),
        ),
        out_specs=(P("rep", "feat", None), P(None, "feat", None), P()),
        check_vma=False,
    )
```

profile of v0, /device:TPU:2, one launch (start us, length us, event | category | flops | bytes accessed | tf_op | source)
XLA Modules:
  0.0 702.0 jit_solution(11061386898485496683)
XLA Ops:
  12.6 151.7 %while.11 = (s32[]{:T(128)}, bf16[8,2,4,512]{3,1,2,0:T(2,128)(2,1)S(1)}, s32[8,15,4,512]{3,2,0,1:T(4,128)S(1)}, bf16[8,2,4,1024]{3,1,2,0:T(2,128)(2,1)S(1)}, s32[]{:T(128)}) while((s32[]{:T(128)}, bf16[8,2,4,512]{3,1,2,0:T(2,128)(2,1)S(1)}, s32[8,15,4,512]{3,2,0,1:T(4,128)S(1)}, bf16[8,2,4,1024]{3,1,2,0:T(2,128)(2,1)S(1)}, s32[]{:T(128)}) %tuple.63), condition=%wide.region_1.2_spmd, body=%wide.region_0.1_spmd.sunk | while | flops 134225920 | bytes 671825 | solution.py:54
  12.7 18.9 %fusion.123 = bf16[8,2,4,512]{3,1,2,0:T(2,128)(2,1)S(1)} fusion(bf16[8,2,4,512]{3,1,2,0:T(2,128)(2,1)S(1)} %get-tuple-element.144, s32[]{:T(128)S(6)} %copy.35, s32[4,512]{1,0:T(4,128)S(1)} %get-tuple-element.123, s32[4,512]{1,0:T(4,128)S(1)} %get-tuple-element.124, s32[4,512]{1,0:T(4,128)S(1)} %get-tuple-element.125, ...), kind=kOutput, calls=%fused_computation.85.clone.3 | convolution fusion | flops 134225920 | bytes 147460 | tf_op jit(solution)/shard_map/while/body/eval_jaxpr/cgs,gvs->cgv/dot_general | solution.py:51
  31.6 18.9 %fusion.123 = bf16[8,2,4,512]{3,1,2,0:T(2,128)(2,1)S(1)} fusion(bf16[8,2,4,512]{3,1,2,0:T(2,128)(2,1)S(1)} %get-tuple-element.144, s32[]{:T(128)S(6)} %copy.35, s32[4,512]{1,0:T(4,128)S(1)} %get-tuple-element.123, s32[4,512]{1,0:T(4,128)S(1)} %get-tuple-element.124, s32[4,512]{1,0:T(4,128)S(1)} %get-tuple-element.125, ...), kind=kOutput, calls=%fused_computation.85.clone.3 | convolution fusion | flops 134225920 | bytes 147460 | tf_op jit(solution)/shard_map/while/body/eval_jaxpr/cgs,gvs->cgv/dot_general | solution.py:51
  50.6 18.9 %fusion.123 = bf16[8,2,4,512]{3,1,2,0:T(2,128)(2,1)S(1)} fusion(bf16[8,2,4,512]{3,1,2,0:T(2,128)(2,1)S(1)} %get-tuple-element.144, s32[]{:T(128)S(6)} %copy.35, s32[4,512]{1,0:T(4,128)S(1)} %get-tuple-element.123, s32[4,512]{1,0:T(4,128)S(1)} %get-tuple-element.124, s32[4,512]{1,0:T(4,128)S(1)} %get-tuple-element.125, ...), kind=kOutput, calls=%fused_computation.85.clone.3 | convolution fusion | flops 134225920 | bytes 147460 | tf_op jit(solution)/shard_map/while/body/eval_jaxpr/cgs,gvs->cgv/dot_general | solution.py:51
  69.5 18.9 %fusion.123 = bf16[8,2,4,512]{3,1,2,0:T(2,128)(2,1)S(1)} fusion(bf16[8,2,4,512]{3,1,2,0:T(2,128)(2,1)S(1)} %get-tuple-element.144, s32[]{:T(128)S(6)} %copy.35, s32[4,512]{1,0:T(4,128)S(1)} %get-tuple-element.123, s32[4,512]{1,0:T(4,128)S(1)} %get-tuple-element.124, s32[4,512]{1,0:T(4,128)S(1)} %get-tuple-element.125, ...), kind=kOutput, calls=%fused_computation.85.clone.3 | convolution fusion | flops 134225920 | bytes 147460 | tf_op jit(solution)/shard_map/while/body/eval_jaxpr/cgs,gvs->cgv/dot_general | solution.py:51
  88.5 18.9 %fusion.123 = bf16[8,2,4,512]{3,1,2,0:T(2,128)(2,1)S(1)} fusion(bf16[8,2,4,512]{3,1,2,0:T(2,128)(2,1)S(1)} %get-tuple-element.144, s32[]{:T(128)S(6)} %copy.35, s32[4,512]{1,0:T(4,128)S(1)} %get-tuple-element.123, s32[4,512]{1,0:T(4,128)S(1)} %get-tuple-element.124, s32[4,512]{1,0:T(4,128)S(1)} %get-tuple-element.125, ...), kind=kOutput, calls=%fused_computation.85.clone.3 | convolution fusion | flops 134225920 | bytes 147460 | tf_op jit(solution)/shard_map/while/body/eval_jaxpr/cgs,gvs->cgv/dot_general | solution.py:51
  107.5 18.9 %fusion.123 = bf16[8,2,4,512]{3,1,2,0:T(2,128)(2,1)S(1)} fusion(bf16[8,2,4,512]{3,1,2,0:T(2,128)(2,1)S(1)} %get-tuple-element.144, s32[]{:T(128)S(6)} %copy.35, s32[4,512]{1,0:T(4,128)S(1)} %get-tuple-element.123, s32[4,512]{1,0:T(4,128)S(1)} %get-tuple-element.124, s32[4,512]{1,0:T(4,128)S(1)} %get-tuple-element.125, ...), kind=kOutput, calls=%fused_computation.85.clone.3 | convolution fusion | flops 134225920 | bytes 147460 | tf_op jit(solution)/shard_map/while/body/eval_jaxpr/cgs,gvs->cgv/dot_general | solution.py:51
  126.4 18.9 %fusion.123 = bf16[8,2,4,512]{3,1,2,0:T(2,128)(2,1)S(1)} fusion(bf16[8,2,4,512]{3,1,2,0:T(2,128)(2,1)S(1)} %get-tuple-element.144, s32[]{:T(128)S(6)} %copy.35, s32[4,512]{1,0:T(4,128)S(1)} %get-tuple-element.123, s32[4,512]{1,0:T(4,128)S(1)} %get-tuple-element.124, s32[4,512]{1,0:T(4,128)S(1)} %get-tuple-element.125, ...), kind=kOutput, calls=%fused_computation.85.clone.3 | convolution fusion | flops 134225920 | bytes 147460 | tf_op jit(solution)/shard_map/while/body/eval_jaxpr/cgs,gvs->cgv/dot_general | solution.py:51
  145.4 18.9 %fusion.123 = bf16[8,2,4,512]{3,1,2,0:T(2,128)(2,1)S(1)} fusion(bf16[8,2,4,512]{3,1,2,0:T(2,128)(2,1)S(1)} %get-tuple-element.144, s32[]{:T(128)S(6)} %copy.35, s32[4,512]{1,0:T(4,128)S(1)} %get-tuple-element.123, s32[4,512]{1,0:T(4,128)S(1)} %get-tuple-element.124, s32[4,512]{1,0:T(4,128)S(1)} %get-tuple-element.125, ...), kind=kOutput, calls=%fused_computation.85.clone.3 | convolution fusion | flops 134225920 | bytes 147460 | tf_op jit(solution)/shard_map/while/body/eval_jaxpr/cgs,gvs->cgv/dot_general | solution.py:51
  164.5 12.9 %copy.17 = bf16[2,2,16384]{1,0,2:T(2,128)(2,1)} copy(bf16[2,2,16384]{2,1,0:T(2,128)(2,1)S(1)} %pad_maximum_fusion.2) | data formatting | bytes 262144 | tf_op jit(solution)/shard_map/stack | solution.py:69
  177.5 13.7 %reshape.627 = bf16[64,2,512]{2,1,0:T(2,128)(2,1)} reshape(bf16[16384,2,2]{2,1,0:T(2,128)(2,1)} %bitcast.148) | data formatting | bytes 262144
  191.2 12.0 %all-to-all-start = ((bf16[64,2,512]{2,1,0:T(2,128)(2,1)}), bf16[64,2,512]{2,1,0:T(2,128)(2,1)S(1)}, u32[]{:S(2)}, u32[]{:S(2)}) async-start(bf16[64,2,512]{2,1,0:T(2,128)(2,1)} %reshape.627), calls=%async_computation | async-start | bytes 262144 | tf_op jit(solution)/shard_map/all_to_all | solution.py:19
  203.5 49.5 %all_gather.6 = bf16[2,128,256]{2,0,1:T(2,128)(2,1)S(1)} all-gather(bf16[2,2,256]{2,0,1:T(2,128)(2,1)S(1)} %copy.19), channel_id=1, replica_groups=mesh['feat'=64,'rep'=4] {'feat'}, dimensions={1}, use_global_device_ids=true | all-gather | bytes 133120 | tf_op jit(solution)/shard_map/all_gather | solution.py:72
  253.0 19.1 %reshape.628 = bf16[16384,2,2]{2,1,0:T(2,128)(2,1)} reshape(bf16[64,2,512]{2,1,0:T(2,128)(2,1)S(1)} %all-to-all-done) | data formatting | bytes 262144
  272.0 16.5 %copy.18 = bf16[2,2,64,256]{3,0,1,2:T(2,128)(2,1)S(1)} copy(bf16[2,2,64,256]{1,0,3,2:T(2,128)(2,1)} %bitcast.149) | data formatting | bytes 262144 | tf_op jit(solution)/shard_map/all_to_all | solution.py:19
  289.5 7.5 %gather_fusion = bf16[2048,256]{1,0:T(8,128)(2,1)S(1)} fusion(bf16[256,256]{1,0:T(8,128)(2,1)S(1)} %get-tuple-element.81, s32[2048]{0:T(1024)S(1)} %broadcast_clamp_fusion), kind=kCustom, calls=%fused_computation | custom fusion | bytes 2105344 | tf_op jit(solution)/shard_map/gather | solution.py:80
  298.3 9.2 %all-to-all-start.1 = ((bf16[64,32,256]{2,1,0:T(8,128)(2,1)}), bf16[64,32,256]{2,1,0:T(8,128)(2,1)S(1)}, u32[]{:S(2)}, u32[]{:S(2)}) async-start(bf16[64,32,256]{2,1,0:T(8,128)(2,1)} %broadcast_select_fusion), calls=%async_computation.1 | async-start | bytes 2097152 | tf_op jit(solution)/shard_map/all_to_all | solution.py:82
  307.9 26.5 %all-to-all-done.1 = bf16[64,32,256]{2,1,0:T(8,128)(2,1)S(1)} async-done(((bf16[64,32,256]{2,1,0:T(8,128)(2,1)}), bf16[64,32,256]{2,1,0:T(8,128)(2,1)S(1)}, u32[]{:S(2)}, u32[]{:S(2)}) %all-to-all-start.1) | async-done | bytes 1048608 | tf_op jit(solution)/shard_map/all_to_all | solution.py:82
  377.5 8.0 %all-to-all-start.2 = ((bf16[64,32,256]{2,1,0:T(8,128)(2,1)}), bf16[64,32,256]{2,1,0:T(8,128)(2,1)}, u32[]{:S(2)}, u32[]{:S(2)}) async-start(bf16[64,32,256]{2,1,0:T(8,128)(2,1)} %bitcast.57), calls=%async_computation.2 | async-start | bytes 2097152 | tf_op jit(solution)/shard_map/all_to_all | solution.py:119
  385.7 26.6 %all-to-all-done.2 = bf16[64,32,256]{2,1,0:T(8,128)(2,1)} async-done(((bf16[64,32,256]{2,1,0:T(8,128)(2,1)}), bf16[64,32,256]{2,1,0:T(8,128)(2,1)}, u32[]{:S(2)}, u32[]{:S(2)}) %all-to-all-start.2) | async-done | bytes 1048608 | tf_op jit(solution)/shard_map/all_to_all | solution.py:119
  413.9 11.9 %scatter_fusion.9 = f32[256,256]{1,0:T(8,128)S(1)} fusion(f32[256,256]{1,0:T(8,128)S(1)} %convolution_add_fusion, s32[2048]{0:T(1024)S(1)} %reshape.446, f32[2048,256]{1,0:T(8,128)S(1)} %bitcast.150), kind=kCustom, calls=%fused_computation.21 | custom fusion | flops 524288 | bytes 6299648 | tf_op jit(solution)/shard_map/scatter-add | solution.py:127
  427.9 79.4 %all-gather.2.cloned.1.call-done = bf16[16384,256]{1,0:T(8,128)(2,1)} async-done(((bf16[256,256]{1,0:T(8,128)(2,1)}), bf16[16384,256]{1,0:T(8,128)(2,1)}) %all-gather.2.cloned.1.call-update) | async-done | bytes 8388624 | tf_op jit(solution)/shard_map/all_gather | solution.py:132
  512.0 11.0 %psum.14 = f32[2,2,256]{2,1,0:T(2,128)} all-reduce(f32[2,2,256]{2,1,0:T(2,128)S(1)} %fusion.75), channel_id=1, replica_groups=mesh['feat'=64,'rep'=4] {'rep'}, use_global_device_ids=true, to_apply=%region_13.14 | all-reduce | flops 1024 | bytes 8192 | tf_op jit(solution)/shard_map/psum | solution.py:135
  523.0 169.4 %all-reduce.2.cloned.1.call-done = f32[2,256,256]{2,1,0:T(8,128)} async-done(((f32[2,256,256]{2,1,0:T(8,128)}), f32[2,256,256]{2,1,0:T(8,128)}) %all-reduce.2.cloned.1.call-update) | async-done | bytes 524304 | tf_op jit(solution)/shard_map/psum | solution.py:107
  (103 shorter events, 61.5 us)
Async XLA Ops:
  8.0 4.6 copy-start.2
  177.4 25.8 %copy-start.3 = (s32[1,1,64,32]{2,3,1,0:T(8,128)S(1)}, s32[1,1,64,32]{2,3,1,0:T(8,128)}, u32[]{:S(2)}) copy-start(s32[1,1,64,32]{2,3,1,0:T(8,128)} %param.16) | copy-start | bytes 24580
  177.4 25.8 %copy-start.6 = (s32[1,1,64]{2,1,0:T(1,128)S(1)}, s32[1,1,64]{2,1,0:T(1,128)}, u32[]{:S(2)}) copy-start(s32[1,1,64]{2,1,0:T(1,128)} %param.17) | copy-start | bytes 772
  177.5 25.9 %copy-start.5 = (bf16[2,2,256]{2,1,0:T(2,128)(2,1)S(1)}, bf16[2,2,256]{2,1,0:T(2,128)(2,1)}, u32[]{:S(2)}) copy-start(bf16[2,2,256]{2,1,0:T(2,128)(2,1)} %param.14) | copy-start | bytes 6148
  191.2 61.8 %all-to-all-start = ((bf16[64,2,512]{2,1,0:T(2,128)(2,1)}), bf16[64,2,512]{2,1,0:T(2,128)(2,1)S(1)}, u32[]{:S(2)}, u32[]{:S(2)}) async-start(bf16[64,2,512]{2,1,0:T(2,128)(2,1)} %reshape.627), calls=%async_computation | async-start | bytes 262144 | tf_op jit(solution)/shard_map/all_to_all | solution.py:19
  297.0 10.5 %copy-start.4 = (s32[1,10,256]{2,0,1:T(1,128)S(1)}, s32[1,10,256]{2,0,1:T(1,128)}, u32[]{:S(2)}) copy-start(s32[1,10,256]{2,0,1:T(1,128)} %param.18) | copy-start | bytes 30724
  297.0 10.7 %copy-start = (bf16[2,256,256]{2,1,0:T(8,128)(2,1)S(1)}, bf16[2,256,256]{2,1,0:T(8,128)(2,1)}, u32[]{:S(2)}) copy-start(bf16[2,256,256]{2,1,0:T(8,128)(2,1)} %param.15) | copy-start | bytes 786436
  298.3 36.0 %all-to-all-start.1 = ((bf16[64,32,256]{2,1,0:T(8,128)(2,1)}), bf16[64,32,256]{2,1,0:T(8,128)(2,1)S(1)}, u32[]{:S(2)}, u32[]{:S(2)}) async-start(bf16[64,32,256]{2,1,0:T(8,128)(2,1)} %broadcast_select_fusion), calls=%async_computation.1 | async-start | bytes 2097152 | tf_op jit(solution)/shard_map/all_to_all | solution.py:82
  377.5 34.8 %all-to-all-start.2 = ((bf16[64,32,256]{2,1,0:T(8,128)(2,1)}), bf16[64,32,256]{2,1,0:T(8,128)(2,1)}, u32[]{:S(2)}, u32[]{:S(2)}) async-start(bf16[64,32,256]{2,1,0:T(8,128)(2,1)} %bitcast.57), calls=%async_computation.2 | async-start | bytes 2097152 | tf_op jit(solution)/shard_map/all_to_all | solution.py:119
  385.5 121.8 %all-gather.2.cloned.1.call-start = ((), (), s32[]{:S(2)}) async-start(), calls=%async_computation.3 | async-start | bytes 8519680 | tf_op jit(solution)/shard_map/all_gather | solution.py:132
  413.9 11.9 %copy-start.1 = (f32[256,256]{1,0:T(8,128)S(1)}, f32[256,256]{1,0:T(8,128)}, u32[]{:S(2)}) copy-start(f32[256,256]{1,0:T(8,128)} %get-tuple-element.82) | copy-start | bytes 786436
  426.6 265.9 %all-reduce.2.cloned.1.call-start = ((), (), s32[]{:S(2)}) async-start(), calls=%async_computation.4 | async-start | bytes 1048576 | tf_op jit(solution)/shard_map/psum | solution.py:107
Sparse Core Ops, SparseCore 0:
  426.7 80.5 all-gather.1
Sparse Core Ops, SparseCore 1:
  433.1 259.3 all-reduce.1
where the time goes:
time: 711 us; the launch traced here: 702 us
  waiting for transfers between devices  302 us (42%)
  matrix products  160 us (23%)
  local copies, waits for them, and re-layouts  85.5 us (12%)
  blocking collectives  60.5 us (9%)
  other arithmetic  48.8 us (7%)
  starting transfers between devices  29.3 us (4%)
  between operations  16.1 us (2%)
    psum x1, waiting for transfers between devices, on_device(): grad_two = lax.psum(local_two, ('feat', 'rep'))  169 us
    dot_general x8, matrix products, one_turn(): jnp.einsum('cgs,gvs->cgv', table_part, tallies, preferred_element_type=jn...  151 us
    all_gather x1, waiting for transfers between devices, on_device(): lax.all_gather(slope_one, 'feat', axis=0, tiled=True)  79.4 us
    all_gather x1, blocking collectives, on_device(): full_weight = lax.all_gather(weight_one, 'feat', axis=1, tiled=True)  49.5 us
    unnamed x18, local copies, waits for them, and re-layouts  34.7 us
    scatter-add x10, other arithmetic, on_device(): grad_table = grad_table.at[index_two[sample]].add(back_agg)  28.1 us
    all_to_all x1, waiting for transfers between devices, on_device(): lax.all_to_all(grad_table[node_count:].reshape(feat_devs, capacity, hidde...  26.6 us
    all_to_all x1, waiting for transfers between devices, on_device(): lax.all_to_all(outgoing, 'feat', split_axis=0, concat_axis=0, tiled=True)  26.5 us
  transfers between devices with their start and end apart: 5, of which 4 were waited for; matrix products, arithmetic and copies ran while one was open for 1% of the time, Pallas kernels for 0%

commit v1 on v0

--- a/solution.py
+++ b/solution.py
@@ -1,10 +1,22 @@
+import functools
 import math
 import jax
 import jax.numpy as jnp
 from jax import lax
 from jax.sharding import PartitionSpec as P
+from jax.lax import all_to_all, axis_size
 
 BLOCK_NODES = 512
+
+
+def form_strings(matrix, across, pos_dim):
+    main = jnp.stack([matrix for _ in range(axis_size(across))], 0)
+    row_out = all_to_all(main, across, 0, 0)
+    placed = jnp.concatenate(row_out, pos_dim)
+    return placed
+
+
+reach_the_screen = functools.partial(form_strings, across="feat", pos_dim=1)
 
 
 def activate(pre):
@@ -69,7 +81,7 @@
     stacked = jnp.stack([table_x[:, :layer_rows], aggregate_one])
     node_feats = None
     node_feats = to_nodes(stacked)
-    full_weight = lax.all_gather(weight_one, "feat", axis=1, tiled=True)
+    full_weight = reach_the_screen(weight_one)
     pre_one = jnp.einsum("sfr,sfh->rh", node_feats, full_weight, preferred_element_type=jnp.float32)
     hidden_one = activate(pre_one).astype(jnp.bfloat16)
     send_slots = send_rows[0, 0]

time: 711 us -> 679 us (0.955)
  blocking collectives: 60.5 us -> 11.1 us
  waiting for transfers between devices: 302 us -> 310 us
    all_gather x1 -> x0, blocking collectives: 49.5 us -> none  [on_device(): full_weight = lax.all_gather(weight_one, 'feat', axis=1, tiled=True)]
    all_to_all x0 -> x1, starting transfers between devices: none -> 12 us  [form_strings(): row_out = all_to_all(main, across, 0, 0)]
    all_to_all x1, waiting for transfers between devices: 0.01 us -> 8.95 us  [to_nodes(): lax.all_to_all(stacked, 'feat', split_axis=2, concat_axis=1, tiled=True)]
    unnamed x18 -> x15, local copies, waits for them, and re-layouts: 34.7 us -> 34.6 us
  transfers between devices with their start and end apart: 5 -> 6, of which waited for: 4 -> 5; matrix products, arithmetic and copies ran while one was open for 1% -> 28% of each run, Pallas kernels for 0% -> 0%
where the time goes in v1:
time: 679 us; the launch traced here: 670 us
  waiting for transfers between devices  310 us (46%)
  matrix products  160 us (24%)
  local copies, waits for them, and re-layouts  87.1 us (13%)
  other arithmetic  48.8 us (7%)
  starting transfers between devices  36.4 us (5%)
  between operations  16.1 us (2%)
  blocking collectives  11.1 us (2%)
    psum x1, waiting for transfers between devices, on_device(): grad_two = lax.psum(local_two, ('feat', 'rep'))  169 us
    dot_general x8, matrix products, one_turn(): jnp.einsum('cgs,gvs->cgv', table_part, tallies, preferred_element_type=jn...  151 us
    all_gather x1, waiting for transfers between devices, on_device(): lax.all_gather(slope_one, 'feat', axis=0, tiled=True)  79.4 us
    unnamed x15, local copies, waits for them, and re-layouts  34.6 us
    scatter-add x10, other arithmetic, on_device(): grad_table = grad_table.at[index_two[sample]].add(back_agg)  28.1 us
    all_to_all x1, waiting for transfers between devices, on_device(): lax.all_to_all(outgoing, 'feat', split_axis=0, concat_axis=0, tiled=True)  26.6 us
    all_to_all x1, waiting for transfers between devices, on_device(): lax.all_to_all(grad_table[node_count:].reshape(feat_devs, capacity, hidde...  26.6 us
    all_to_all x1, local copies, waits for them, and re-layouts, to_nodes(): lax.all_to_all(stacked, 'feat', split_axis=2, concat_axis=1, tiled=True)  16.5 us
  transfers between devices with their start and end apart: 6, of which 5 were waited for; matrix products, arithmetic and copies ran while one was open for 28% of the time, Pallas kernels for 0%

profile of v1, /device:TPU:2, one launch (start us, length us, event | category | flops | bytes accessed | tf_op | source)
XLA Modules:
  0.0 669.8 jit_solution(10001107616610785118)
XLA Ops:
  9.4 12.0 %all-to-all-start.1 = ((bf16[64,2,2,256]{3,2,1,0:T(2,128)(2,1)}), bf16[64,2,2,256]{3,2,1,0:T(2,128)(2,1)S(1)}, u32[]{:S(2)}, u32[]{:S(2)}) async-start(bf16[64,2,2,256]{3,2,1,0:T(2,128)(2,1)} %stack.14), calls=%async_computation.1 | async-start | bytes 262144 | tf_op jit(solution)/shard_map/all_to_all | solution.py:14
  26.0 151.7 %while.11 = (s32[]{:T(128)}, bf16[8,2,4,512]{3,1,2,0:T(2,128)(2,1)S(1)}, s32[8,15,4,512]{3,2,0,1:T(4,128)S(1)}, bf16[8,2,4,1024]{3,1,2,0:T(2,128)(2,1)S(1)}, s32[]{:T(128)}) while((s32[]{:T(128)}, bf16[8,2,4,512]{3,1,2,0:T(2,128)(2,1)S(1)}, s32[8,15,4,512]{3,2,0,1:T(4,128)S(1)}, bf16[8,2,4,1024]{3,1,2,0:T(2,128)(2,1)S(1)}, s32[]{:T(128)}) %tuple.63), condition=%wide.region_1.2_spmd, body=%wide.region_0.1_spmd.sunk | while | flops 134225920 | bytes 671825 | solution.py:66
  26.1 18.9 %fusion.123 = bf16[8,2,4,512]{3,1,2,0:T(2,128)(2,1)S(1)} fusion(bf16[8,2,4,512]{3,1,2,0:T(2,128)(2,1)S(1)} %get-tuple-element.144, s32[]{:T(128)S(6)} %copy.30, s32[4,512]{1,0:T(4,128)S(1)} %get-tuple-element.123, s32[4,512]{1,0:T(4,128)S(1)} %get-tuple-element.124, s32[4,512]{1,0:T(4,128)S(1)} %get-tuple-element.125, ...), kind=kOutput, calls=%fused_computation.85.clone.3 | convolution fusion | flops 134225920 | bytes 147460 | tf_op jit(solution)/shard_map/while/body/eval_jaxpr/cgs,gvs->cgv/dot_general | solution.py:63
  45.1 18.9 %fusion.123 = bf16[8,2,4,512]{3,1,2,0:T(2,128)(2,1)S(1)} fusion(bf16[8,2,4,512]{3,1,2,0:T(2,128)(2,1)S(1)} %get-tuple-element.144, s32[]{:T(128)S(6)} %copy.30, s32[4,512]{1,0:T(4,128)S(1)} %get-tuple-element.123, s32[4,512]{1,0:T(4,128)S(1)} %get-tuple-element.124, s32[4,512]{1,0:T(4,128)S(1)} %get-tuple-element.125, ...), kind=kOutput, calls=%fused_computation.85.clone.3 | convolution fusion | flops 134225920 | bytes 147460 | tf_op jit(solution)/shard_map/while/body/eval_jaxpr/cgs,gvs->cgv/dot_general | solution.py:63
  64.0 18.9 %fusion.123 = bf16[8,2,4,512]{3,1,2,0:T(2,128)(2,1)S(1)} fusion(bf16[8,2,4,512]{3,1,2,0:T(2,128)(2,1)S(1)} %get-tuple-element.144, s32[]{:T(128)S(6)} %copy.30, s32[4,512]{1,0:T(4,128)S(1)} %get-tuple-element.123, s32[4,512]{1,0:T(4,128)S(1)} %get-tuple-element.124, s32[4,512]{1,0:T(4,128)S(1)} %get-tuple-element.125, ...), kind=kOutput, calls=%fused_computation.85.clone.3 | convolution fusion | flops 134225920 | bytes 147460 | tf_op jit(solution)/shard_map/while/body/eval_jaxpr/cgs,gvs->cgv/dot_general | solution.py:63
  83.0 18.9 %fusion.123 = bf16[8,2,4,512]{3,1,2,0:T(2,128)(2,1)S(1)} fusion(bf16[8,2,4,512]{3,1,2,0:T(2,128)(2,1)S(1)} %get-tuple-element.144, s32[]{:T(128)S(6)} %copy.30, s32[4,512]{1,0:T(4,128)S(1)} %get-tuple-element.123, s32[4,512]{1,0:T(4,128)S(1)} %get-tuple-element.124, s32[4,512]{1,0:T(4,128)S(1)} %get-tuple-element.125, ...), kind=kOutput, calls=%fused_computation.85.clone.3 | convolution fusion | flops 134225920 | bytes 147460 | tf_op jit(solution)/shard_map/while/body/eval_jaxpr/cgs,gvs->cgv/dot_general | solution.py:63
  102.0 18.9 %fusion.123 = bf16[8,2,4,512]{3,1,2,0:T(2,128)(2,1)S(1)} fusion(bf16[8,2,4,512]{3,1,2,0:T(2,128)(2,1)S(1)} %get-tuple-element.144, s32[]{:T(128)S(6)} %copy.30, s32[4,512]{1,0:T(4,128)S(1)} %get-tuple-element.123, s32[4,512]{1,0:T(4,128)S(1)} %get-tuple-element.124, s32[4,512]{1,0:T(4,128)S(1)} %get-tuple-element.125, ...), kind=kOutput, calls=%fused_computation.85.clone.3 | convolution fusion | flops 134225920 | bytes 147460 | tf_op jit(solution)/shard_map/while/body/eval_jaxpr/cgs,gvs->cgv/dot_general | solution.py:63
  120.9 18.9 %fusion.123 = bf16[8,2,4,512]{3,1,2,0:T(2,128)(2,1)S(1)} fusion(bf16[8,2,4,512]{3,1,2,0:T(2,128)(2,1)S(1)} %get-tuple-element.144, s32[]{:T(128)S(6)} %copy.30, s32[4,512]{1,0:T(4,128)S(1)} %get-tuple-element.123, s32[4,512]{1,0:T(4,128)S(1)} %get-tuple-element.124, s32[4,512]{1,0:T(4,128)S(1)} %get-tuple-element.125, ...), kind=kOutput, calls=%fused_computation.85.clone.3 | convolution fusion | flops 134225920 | bytes 147460 | tf_op jit(solution)/shard_map/while/body/eval_jaxpr/cgs,gvs->cgv/dot_general | solution.py:63
  139.9 18.9 %fusion.123 = bf16[8,2,4,512]{3,1,2,0:T(2,128)(2,1)S(1)} fusion(bf16[8,2,4,512]{3,1,2,0:T(2,128)(2,1)S(1)} %get-tuple-element.144, s32[]{:T(128)S(6)} %copy.30, s32[4,512]{1,0:T(4,128)S(1)} %get-tuple-element.123, s32[4,512]{1,0:T(4,128)S(1)} %get-tuple-element.124, s32[4,512]{1,0:T(4,128)S(1)} %get-tuple-element.125, ...), kind=kOutput, calls=%fused_computation.85.clone.3 | convolution fusion | flops 134225920 | bytes 147460 | tf_op jit(solution)/shard_map/while/body/eval_jaxpr/cgs,gvs->cgv/dot_general | solution.py:63
  158.9 18.9 %fusion.123 = bf16[8,2,4,512]{3,1,2,0:T(2,128)(2,1)S(1)} fusion(bf16[8,2,4,512]{3,1,2,0:T(2,128)(2,1)S(1)} %get-tuple-element.144, s32[]{:T(128)S(6)} %copy.30, s32[4,512]{1,0:T(4,128)S(1)} %get-tuple-element.123, s32[4,512]{1,0:T(4,128)S(1)} %get-tuple-element.124, s32[4,512]{1,0:T(4,128)S(1)} %get-tuple-element.125, ...), kind=kOutput, calls=%fused_computation.85.clone.3 | convolution fusion | flops 134225920 | bytes 147460 | tf_op jit(solution)/shard_map/while/body/eval_jaxpr/cgs,gvs->cgv/dot_general | solution.py:63
  178.0 12.9 %copy.17 = bf16[2,2,16384]{1,0,2:T(2,128)(2,1)} copy(bf16[2,2,16384]{2,1,0:T(2,128)(2,1)S(1)} %pad_maximum_fusion.2) | data formatting | bytes 262144 | tf_op jit(solution)/shard_map/stack | solution.py:81
  190.9 13.7 %reshape.637 = bf16[64,2,512]{2,1,0:T(2,128)(2,1)} reshape(bf16[16384,2,2]{2,1,0:T(2,128)(2,1)} %bitcast.150) | data formatting | bytes 262144
  204.7 10.3 %all-to-all-start = ((bf16[64,2,512]{2,1,0:T(2,128)(2,1)}), bf16[64,2,512]{2,1,0:T(2,128)(2,1)S(1)}, u32[]{:S(2)}, u32[]{:S(2)}) async-start(bf16[64,2,512]{2,1,0:T(2,128)(2,1)} %reshape.637), calls=%async_computation | async-start | bytes 262144 | tf_op jit(solution)/shard_map/all_to_all | solution.py:31
  215.4 9.0 %all-to-all-done = bf16[64,2,512]{2,1,0:T(2,128)(2,1)S(1)} async-done(((bf16[64,2,512]{2,1,0:T(2,128)(2,1)}), bf16[64,2,512]{2,1,0:T(2,128)(2,1)S(1)}, u32[]{:S(2)}, u32[]{:S(2)}) %all-to-all-start) | async-done | bytes 131104 | tf_op jit(solution)/shard_map/all_to_all | solution.py:31
  224.4 19.0 %reshape.638 = bf16[16384,2,2]{2,1,0:T(2,128)(2,1)} reshape(bf16[64,2,512]{2,1,0:T(2,128)(2,1)S(1)} %all-to-all-done) | data formatting | bytes 262144
  243.4 16.5 %copy.18 = bf16[2,2,64,256]{3,0,1,2:T(2,128)(2,1)S(1)} copy(bf16[2,2,64,256]{1,0,3,2:T(2,128)(2,1)} %bitcast.151) | data formatting | bytes 262144 | tf_op jit(solution)/shard_map/all_to_all | solution.py:31
  260.9 7.5 %gather_fusion = bf16[2048,256]{1,0:T(8,128)(2,1)S(1)} fusion(bf16[256,256]{1,0:T(8,128)(2,1)S(1)} %get-tuple-element.81, s32[2048]{0:T(1024)S(1)} %broadcast_clamp_fusion), kind=kCustom, calls=%fused_computation | custom fusion | bytes 2105344 | tf_op jit(solution)/shard_map/gather | solution.py:92
  276.0 26.6 %all-to-all-done.2 = bf16[64,32,256]{2,1,0:T(8,128)(2,1)S(1)} async-done(((bf16[64,32,256]{2,1,0:T(8,128)(2,1)}), bf16[64,32,256]{2,1,0:T(8,128)(2,1)S(1)}, u32[]{:S(2)}, u32[]{:S(2)}) %all-to-all-start.2) | async-done | bytes 1048608 | tf_op jit(solution)/shard_map/all_to_all | solution.py:94
  345.8 8.0 %all-to-all-start.3 = ((bf16[64,32,256]{2,1,0:T(8,128)(2,1)}), bf16[64,32,256]{2,1,0:T(8,128)(2,1)}, u32[]{:S(2)}, u32[]{:S(2)}) async-start(bf16[64,32,256]{2,1,0:T(8,128)(2,1)} %bitcast.58), calls=%async_computation.3 | async-start | bytes 2097152 | tf_op jit(solution)/shard_map/all_to_all | solution.py:131
  354.1 26.6 %all-to-all-done.3 = bf16[64,32,256]{2,1,0:T(8,128)(2,1)} async-done(((bf16[64,32,256]{2,1,0:T(8,128)(2,1)}), bf16[64,32,256]{2,1,0:T(8,128)(2,1)}, u32[]{:S(2)}, u32[]{:S(2)}) %all-to-all-start.3) | async-done | bytes 1048608 | tf_op jit(solution)/shard_map/all_to_all | solution.py:131
  382.2 11.9 %scatter_fusion.9 = f32[256,256]{1,0:T(8,128)S(1)} fusion(f32[256,256]{1,0:T(8,128)S(1)} %convolution_add_fusion, s32[2048]{0:T(1024)S(1)} %reshape.456, f32[2048,256]{1,0:T(8,128)S(1)} %bitcast.152), kind=kCustom, calls=%fused_computation.21 | custom fusion | flops 524288 | bytes 6299648 | tf_op jit(solution)/shard_map/scatter-add | solution.py:139
  396.2 79.4 %all-gather.2.cloned.1.call-done = bf16[16384,256]{1,0:T(8,128)(2,1)} async-done(((bf16[256,256]{1,0:T(8,128)(2,1)}), bf16[16384,256]{1,0:T(8,128)(2,1)}) %all-gather.2.cloned.1.call-update) | async-done | bytes 8388624 | tf_op jit(solution)/shard_map/all_gather | solution.py:144
  480.4 11.1 %psum.14 = f32[2,2,256]{2,1,0:T(2,128)} all-reduce(f32[2,2,256]{2,1,0:T(2,128)S(1)} %fusion.75), channel_id=1, replica_groups=mesh['feat'=64,'rep'=4] {'rep'}, use_global_device_ids=true, to_apply=%region_13.14 | all-reduce | flops 1024 | bytes 8192 | tf_op jit(solution)/shard_map/psum | solution.py:147
  491.5 168.8 %all-reduce.2.cloned.1.call-done = f32[2,256,256]{2,1,0:T(8,128)} async-done(((f32[2,256,256]{2,1,0:T(8,128)}), f32[2,256,256]{2,1,0:T(8,128)}) %all-reduce.2.cloned.1.call-update) | async-done | bytes 524304 | tf_op jit(solution)/shard_map/psum | solution.py:119
  (104 shorter events, 69.1 us)
Async XLA Ops:
  8.0 18.0 %copy-start.2 = (bf16[1,2,32768]{2,1,0:T(2,128)(2,1)S(1)}, bf16[1,2,32768]{2,1,0:T(2,128)(2,1)}, u32[]{:S(2)}) copy-start(bf16[1,2,32768]{2,1,0:T(2,128)(2,1)} %param.12) | copy-start | bytes 393220
  9.4 195.2 %all-to-all-start.1 = ((bf16[64,2,2,256]{3,2,1,0:T(2,128)(2,1)}), bf16[64,2,2,256]{3,2,1,0:T(2,128)(2,1)S(1)}, u32[]{:S(2)}, u32[]{:S(2)}) async-start(bf16[64,2,2,256]{3,2,1,0:T(2,128)(2,1)} %stack.14), calls=%async_computation.1 | async-start | bytes 262144 | tf_op jit(solution)/shard_map/all_to_all | solution.py:14
  190.9 13.7 %copy-start.3 = (s32[1,1,64,32]{2,3,1,0:T(8,128)S(1)}, s32[1,1,64,32]{2,3,1,0:T(8,128)}, u32[]{:S(2)}) copy-start(s32[1,1,64,32]{2,3,1,0:T(8,128)} %param.16) | copy-start | bytes 24580
  190.9 24.1 %copy-start.5 = (s32[1,1,64]{2,1,0:T(1,128)S(1)}, s32[1,1,64]{2,1,0:T(1,128)}, u32[]{:S(2)}) copy-start(s32[1,1,64]{2,1,0:T(1,128)} %param.17) | copy-start | bytes 772
  204.7 19.7 %all-to-all-start = ((bf16[64,2,512]{2,1,0:T(2,128)(2,1)}), bf16[64,2,512]{2,1,0:T(2,128)(2,1)S(1)}, u32[]{:S(2)}, u32[]{:S(2)}) async-start(bf16[64,2,512]{2,1,0:T(2,128)(2,1)} %reshape.637), calls=%async_computation | async-start | bytes 262144 | tf_op jit(solution)/shard_map/all_to_all | solution.py:31
  268.4 7.3 %copy-start.4 = (s32[1,10,256]{2,0,1:T(1,128)S(1)}, s32[1,10,256]{2,0,1:T(1,128)}, u32[]{:S(2)}) copy-start(s32[1,10,256]{2,0,1:T(1,128)} %param.18) | copy-start | bytes 30724
  268.4 7.4 %copy-start = (bf16[2,256,256]{2,1,0:T(8,128)(2,1)S(1)}, bf16[2,256,256]{2,1,0:T(8,128)(2,1)}, u32[]{:S(2)}) copy-start(bf16[2,256,256]{2,1,0:T(8,128)(2,1)} %param.15) | copy-start | bytes 786436
  269.6 33.0 %all-to-all-start.2 = ((bf16[64,32,256]{2,1,0:T(8,128)(2,1)}), bf16[64,32,256]{2,1,0:T(8,128)(2,1)S(1)}, u32[]{:S(2)}, u32[]{:S(2)}) async-start(bf16[64,32,256]{2,1,0:T(8,128)(2,1)} %broadcast_select_fusion), calls=%async_computation.2 | async-start | bytes 2097152 | tf_op jit(solution)/shard_map/all_to_all | solution.py:94
  345.8 34.8 %all-to-all-start.3 = ((bf16[64,32,256]{2,1,0:T(8,128)(2,1)}), bf16[64,32,256]{2,1,0:T(8,128)(2,1)}, u32[]{:S(2)}, u32[]{:S(2)}) async-start(bf16[64,32,256]{2,1,0:T(8,128)(2,1)} %bitcast.58), calls=%async_computation.3 | async-start | bytes 2097152 | tf_op jit(solution)/shard_map/all_to_all | solution.py:131
  353.8 121.9 %all-gather.2.cloned.1.call-start = ((), (), s32[]{:S(2)}) async-start(), calls=%async_computation.4 | async-start | bytes 8519680 | tf_op jit(solution)/shard_map/all_gather | solution.py:144
  382.2 11.9 %copy-start.1 = (f32[256,256]{1,0:T(8,128)S(1)}, f32[256,256]{1,0:T(8,128)}, u32[]{:S(2)}) copy-start(f32[256,256]{1,0:T(8,128)} %get-tuple-element.82) | copy-start | bytes 786436
  394.9 265.4 %all-reduce.2.cloned.1.call-start = ((), (), s32[]{:S(2)}) async-start(), calls=%async_computation.5 | async-start | bytes 1048576 | tf_op jit(solution)/shard_map/psum | solution.py:119
Sparse Core Ops, SparseCore 0:
  395.0 80.6 all-gather.1
Sparse Core Ops, SparseCore 1:
  401.4 258.8 all-reduce.1
